TPU v7x, 512 devices: a whole 4x8x8 slice. The times are simulated.
512 devices in a mesh: freq: 8 (over x, core), geo: 64 (over z, y).
Axes of the slice: x: 4, y: 8, z: 8, core: 2. Of those that a mesh axis runs over, the one named last changes fastest.
Arguments:
- energy: float32 [256, 48, 36, 128], P('geo', 'freq'), may hold values from 0.1 to 1.5
- water_depth: float32 [256, 128], P('geo'), may hold values from 0.5 to 4
- wet_mask: int32 [256, 128], P('geo'), may hold values 0 or 1
- vegetation: int32 [256, 128], P('geo'), may hold values 0 or 1
- canopy: float32 [256, 128], P('geo'), may hold values from 0.004 to 0.04
- quad_offsets: int32 [4], replicated, may hold values from 1 to 3, as said below
- quad_weights: float32 [2], replicated, may hold values from 0.2 to 0.8
Outputs:
- energy_next: float32 [256, 48, 36, 128], P('geo', 'freq')
- orbital: float32 [256, 128], P('geo')
Inputs may be any that keep to these rules, and one draw needn't show every extreme that they name: `quad_offsets`: offsets a and the two direction turns lie in 1 .. 3; the lower frequency offset b equals 3 in every draw.
All inputs are finite; a program needn't handle non-finite values. No bound on the sum of `wet_mask` or of `vegetation` on one device may be relied on, other than what follows from the above.
Results may differ from a plain program's by a relative error of at most 0.00002.
Values sent between devices are 32-bit elements; how exact they have to be, the bound alone decides.
No kernel may reach another device: no remote copies, remote signals or barrier semaphores. Data moves between devices by JAX's collectives and lax.ppermute only.
A program may use at most 64 MiB of HBM per device.

v0:
```python
import math
import jax
import jax.numpy as jnp
from jax import lax
from jax.sharding import PartitionSpec as P

FH = 4
SUBSTEPS = 8
gravity = 9.81
base_freq = 0.03
freq_ratio = 1.05
cell_size = 20.0
sub_step = 2.0
coupling = 0.01
coef_plus = 0.4096
coef_minus = 3.1605
coef_both = 2.589


def from_neighbour(block, axis, distance, cyclic=False):
    count = lax.axis_size(axis)
    if cyclic:
        pairs = [(i, (i + distance) % count) for i in range(count)]
    else:
        pairs = [(i, i + distance) for i in range(count) if 0 <= i + distance < count]
    return lax.ppermute(block, axis, pairs)


def halo(block, axis, dim, width, side, cyclic=False):
    size = block.shape[dim]
    parts = []
    distance = 1
    need = width
    while need > 0:
        take = min(size, need)
        if side < 0:
            piece = lax.slice_in_dim(block, size - take, size, axis=dim)
            parts.insert(0, from_neighbour(piece, axis, distance, cyclic))
        else:
            piece = lax.slice_in_dim(block, 0, take, axis=dim)
            parts.append(from_neighbour(piece, axis, -distance, cyclic))
        need -= take
        distance += 1
    return parts


def butterfly_sum(value, axis):
    count = lax.axis_size(axis)
    assert count & count - 1 == 0
    step = 1
    while step < count:
        value = value + lax.ppermute(value, axis, [(i, i ^ step) for i in range(count)])
        step *= 2
    return value


def gathered_sum(known, index, count, value):
    reach = max(known)
    if count > 2 * (2 * reach + 1) - 2 or count % 2:
        return butterfly_sum(value, "freq")
    far = count // 2
    ordered = jnp.stack([known[o] for o in range(-reach, reach + 1)])
    more = from_neighbour(ordered, "freq", far, True)
    table = []
    for rel in range(count):
        off = rel if rel <= reach else rel - count
        if -reach <= off <= reach:
            table.append(known[off])
        else:
            table.append(more[rel - far + reach])
    table = jnp.stack(table)
    table = jnp.concatenate([table, table], axis=0)
    start = (count - index) % count
    glob = lax.dynamic_slice_in_dim(table, start, count, axis=0)
    while glob.shape[0] > 1:
        glob = glob[0::2] + glob[1::2]
    return glob[0]


def physics(radian_freq, water_depth, dir_count):
    square = (radian_freq * radian_freq)[None, :, None]
    column = water_depth[:, None, :]
    depth_ratio = square * column / gravity
    depth_wave = depth_ratio / jnp.sqrt(jnp.tanh(depth_ratio))
    group_speed = (
        radian_freq[None, :, None]
        * column
        / depth_wave
        * (0.5 + depth_wave / jnp.sinh(2.0 * depth_wave))
    )
    orbit_weight = (
        square
        / jnp.sinh(depth_wave) ** 2
        * (radian_freq * (freq_ratio - 1.0))[None, :, None]
        * (2.0 * math.pi / dir_count)
    )
    return (group_speed, orbit_weight)


def angles_of(dir_count):
    angles = (jnp.arange(dir_count, dtype=jnp.float32) + 0.5) * (2.0 * math.pi / dir_count)
    return (jnp.cos(angles), jnp.sin(angles))


def shifted(doubled, freq_start, dir_off, count):
    dir_count = doubled.shape[2] // 2
    starts = (jnp.zeros((), jnp.int32), freq_start, dir_off % dir_count, jnp.zeros((), jnp.int32))
    return lax.dynamic_slice(
        doubled, starts, (doubled.shape[0], count, dir_count, doubled.shape[3])
    )


def source_change(extended, quad_offsets, quad_weights, count):
    up_bins, down_bins, up_turn, down_turn = (
        quad_offsets[0],
        quad_offsets[1],
        quad_offsets[2],
        quad_offsets[3],
    )
    weight_up, weight_down = (quad_weights[0], quad_weights[1])
    wide = count + 2 * FH
    doubled = jnp.concatenate([extended, extended], axis=2)
    centre = lax.slice_in_dim(extended, FH, FH + wide, axis=1)
    upper = weight_up * shifted(doubled, FH + up_bins, up_turn, wide) + (1.0 - weight_up) * shifted(
        doubled, FH + up_bins + 1, up_turn, wide
    )
    lower = weight_down * shifted(doubled, FH - down_bins, -down_turn, wide) + (
        1.0 - weight_down
    ) * shifted(doubled, FH - down_bins - 1, -down_turn, wide)
    transfer = coupling * (
        centre * centre * (coef_plus * upper + coef_minus * lower)
        - coef_both * centre * upper * lower
    )
    spread = jnp.concatenate([transfer, transfer], axis=2)
    gained = weight_up * shifted(spread, FH - up_bins, -up_turn, count) + (
        1.0 - weight_up
    ) * shifted(spread, FH - up_bins - 1, -up_turn, count)
    gained = (
        gained
        + weight_down * shifted(spread, FH + down_bins, down_turn, count)
        + (1.0 - weight_down) * shifted(spread, FH + down_bins + 1, down_turn, count)
    )
    own = lax.slice_in_dim(transfer, FH, FH + count, axis=1)
    return gained - 2.0 * own


def east_west(east_flux, cosines):
    zeros = jnp.zeros_like(east_flux[..., :1])
    behind = jnp.concatenate([zeros, east_flux[..., :-1]], axis=-1)
    ahead = jnp.concatenate([east_flux[..., 1:], zeros], axis=-1)
    east_going = (cosines > 0.0)[None, None, :, None]
    return jnp.where(east_going, east_flux - behind, ahead - east_flux)


def propagate(spectrum, speed, wet, cosines, sines, northward):
    step_ratio = sub_step / cell_size
    east_speed = speed[:, :, None, :] * cosines[None, None, :, None]
    north_speed = speed[:, :, None, :] * sines[None, None, :, None]
    rows = spectrum.shape[0]
    for substep in range(SUBSTEPS):
        lo, hi = (substep, rows) if northward else (0, rows - substep)
        east_flux = east_speed[lo:hi] * spectrum
        north_flux = north_speed[lo:hi] * spectrum
        along = north_flux[1:] - north_flux[:-1]
        across = east_west(east_flux, cosines)
        if northward:
            spectrum = wet[lo + 1 : hi, None, None, :] * (
                spectrum[1:] - step_ratio * (across[1:] + along)
            )
        else:
            spectrum = wet[lo : hi - 1, None, None, :] * (
                spectrum[:-1] - step_ratio * (across[:-1] + along)
            )
    return spectrum


def body(energy, water_depth, wet_mask, vegetation, canopy, quad_offsets, quad_weights):
    tile_rows, freq_count, dir_count, tile_cols = energy.shape
    wet_field = wet_mask.astype(jnp.float32)
    veg_field = vegetation.astype(jnp.float32)
    wet_four = wet_field[:, None, None, :]
    masked = wet_four * energy
    first_bin = lax.axis_index("freq") * freq_count
    bin_index = (first_bin + jnp.arange(freq_count, dtype=jnp.int32)).astype(jnp.float32)
    radian_freq = 2.0 * math.pi * base_freq * jnp.power(freq_ratio, bin_index)
    half = dir_count // 2
    cosines, sines = angles_of(dir_count)
    fields = jnp.zeros((tile_rows, 1, half, tile_cols), jnp.float32)
    fields = fields.at[:, 0, 0, :].set(wet_field).at[:, 0, 1, :].set(water_depth)
    north_msg = jnp.concatenate([masked[:, :, :half], fields], axis=1)
    south_msg = jnp.concatenate([masked[:, :, half:], fields], axis=1)
    below = halo(north_msg, "geo", 0, SUBSTEPS, -1)
    above = halo(south_msg, "geo", 0, SUBSTEPS, +1)
    group_speed, orbit_weight = physics(radian_freq, water_depth, dir_count)
    partial_value = jnp.sum(orbit_weight * jnp.sum(energy, axis=2), axis=1)
    freq_index = lax.axis_index("freq")
    freq_total = lax.axis_size("freq")
    slot = jnp.zeros((tile_rows, 1, dir_count, tile_cols), jnp.float32)
    slot = slot.at[:, 0, 0, :].set(partial_value)
    gathered = lax.all_gather(jnp.concatenate([masked, slot], axis=1), "freq", axis=1, tiled=True)
    gathered = gathered.reshape(tile_rows, freq_total, freq_count + 1, dir_count, tile_cols)
    partials = gathered[:, :, freq_count, 0, :]
    spectrum_all = gathered[:, :, :freq_count].reshape(
        tile_rows, freq_total * freq_count, dir_count, tile_cols
    )
    padded_all = jnp.pad(spectrum_all, ((0, 0), (2 * FH, 2 * FH), (0, 0), (0, 0)))
    extended = lax.dynamic_slice_in_dim(padded_all, first_bin, freq_count + 4 * FH, axis=1)
    glob = jnp.moveaxis(partials, 1, 0)
    while glob.shape[0] > 1:
        glob = glob[0::2] + glob[1::2]
    orbital = jnp.sqrt(glob[0])
    full_step = SUBSTEPS * sub_step
    damping = 1.0 + full_step * canopy * veg_field * orbital
    change = source_change(extended, quad_offsets, quad_weights, freq_count)
    increment = (masked + full_step * change) / damping[:, None, None, :] - masked
    geo_index = lax.axis_index("geo")
    geo_count = lax.axis_size("geo")

    def unpack(parts, offsets):
        spectra, speeds, wets = ([], [], [])
        for part, offset in zip(parts, offsets):
            valid = (geo_index + offset >= 0) & (geo_index + offset < geo_count)
            depth = jnp.where(valid, part[:, freq_count, 1, :], 1.0)
            spectra.append(part[:, :freq_count])
            wets.append(part[:, freq_count, 0, :])
            speeds.append(physics(radian_freq, depth, dir_count)[0])
        return (spectra, speeds, wets)

    n_off = [-(len(below) - k) for k in range(len(below))]
    b_spec, b_speed, b_wet = unpack(below, n_off)
    north = propagate(
        jnp.concatenate(b_spec + [masked[:, :, :half]], axis=0),
        jnp.concatenate(b_speed + [group_speed], axis=0),
        jnp.concatenate(b_wet + [wet_field], axis=0),
        cosines[:half],
        sines[:half],
        True,
    )
    s_off = [k + 1 for k in range(len(above))]
    a_spec, a_speed, a_wet = unpack(above, s_off)
    south = propagate(
        jnp.concatenate([masked[:, :, half:]] + a_spec, axis=0),
        jnp.concatenate([group_speed] + a_speed, axis=0),
        jnp.concatenate([wet_field] + a_wet, axis=0),
        cosines[half:],
        sines[half:],
        False,
    )
    moved = jnp.concatenate([north, south], axis=2)
    return (wet_four * (moved + increment), orbital)


def solution(mesh):
    placed = (
        P("geo", "freq", None, None),
        P("geo", None),
        P("geo", None),
        P("geo", None),
        P("geo", None),
        P(),
        P(),
    )
    return jax.shard_map(
        body,
        mesh=mesh,
        in_specs=placed,
        out_specs=(P("geo", "freq", None, None), P("geo", None)),
        check_vma=False,
    )
```

profile of v0, /device:TPU:1, one launch (start us, length us, event | category | flops | bytes accessed | tf_op | source)
XLA Modules:
  0.0 115.2 jit_solution(11909362313528127280)
XLA Ops:
  7.2 0.7 fusion.169
  7.9 1.1 fusion.159
  9.7 1.3 %constant_dynamic-update-slice_fusion = f32[4,1,18,128]{3,0,2,1:T(4,128)S(1)} fusion(f32[4,1,18,128]{3,0,2,1:T(4,128)S(1)} %scatter.10, s32[]{:T(128)} %bitcast.2, f32[4,128]{1,0:T(4,128)} %param.14), kind=kLoop, calls=%fused_computation.258 | loop fusion | bytes 4100 | tf_op jit(solution)/shard_map/scatter | solution.py:189
  11.1 1.3 %collective-permute-start.2 = (f32[4,7,18,128]{3,0,2,1:T(4,128)S(1)}, f32[4,7,18,128]{3,0,2,1:T(4,128)S(1)}, u32[]{:S(2)}, u32[]{:S(2)}) collective-permute-start(f32[4,7,18,128]{3,0,2,1:T(4,128)S(1)} %get-tuple-element.123), channel_id=1, source_target_pairs={{1,0},{2,1},{3,2},{4,3},{5,4},{6,5},{7,6},{8,7},{9,8},{10,9},{11,1... | collective-permute-start | bytes 774152 | tf_op jit(solution)/shard_map/ppermute | solution.py:26
  12.4 1.3 %collective-permute-start.3 = (f32[4,7,18,128]{3,0,2,1:T(4,128)S(1)}, f32[4,7,18,128]{3,0,2,1:T(4,128)S(1)}, u32[]{:S(2)}, u32[]{:S(2)}) collective-permute-start(f32[4,7,18,128]{3,0,2,1:T(4,128)S(1)} %get-tuple-element.123), channel_id=1, source_target_pairs={{2,0},{3,1},{4,2},{5,3},{6,4},{7,5},{8,6},{9,7},{10,8},{11,9},{12,... | collective-permute-start | bytes 774152 | tf_op jit(solution)/shard_map/ppermute | solution.py:26
  13.7 6.5 %collective-permute-start.1 = (f32[4,7,18,128]{3,0,2,1:T(4,128)S(1)}, f32[4,7,18,128]{3,0,2,1:T(4,128)S(1)}, u32[]{:S(2)}, u32[]{:S(2)}) collective-permute-start(f32[4,7,18,128]{3,0,2,1:T(4,128)S(1)} %get-tuple-element.122), channel_id=1, source_target_pairs={{0,2},{1,3},{2,4},{3,5},{4,6},{5,7},{6,8},{7,9},{8,10},{9,11},{10,... | collective-permute-start | bytes 774152 | tf_op jit(solution)/shard_map/ppermute | solution.py:26
  20.2 3.2 %collective-permute-start = (f32[4,7,18,128]{3,0,2,1:T(4,128)S(1)}, f32[4,7,18,128]{3,0,2,1:T(4,128)S(1)}, u32[]{:S(2)}, u32[]{:S(2)}) collective-permute-start(f32[4,7,18,128]{3,0,2,1:T(4,128)S(1)} %get-tuple-element.122), channel_id=1, source_target_pairs={{0,1},{1,2},{2,3},{3,4},{4,5},{5,6},{6,7},{7,8},{8,9},{9,10},{10,1... | collective-permute-start | bytes 774152 | tf_op jit(solution)/shard_map/ppermute | solution.py:26
  24.1 1.3 %fusion.170 = (f32[1]{0:T(128)}, f32[1]{0:T(128)}) fusion(f32[2]{0:T(128)} %param.19), kind=kLoop, calls=%fused_computation.307 | loop fusion | bytes 16 | tf_op jit(solution)/shard_map/slice | solution.py:120
  25.4 1.5 %fusion.171 = (s32[1]{0:T(128)}, s32[1]{0:T(128)}, s32[1]{0:T(128)}, s32[1]{0:T(128)}) fusion(s32[4]{0:T(128)} %param.18), kind=kLoop, calls=%fused_computation.308 | loop fusion | bytes 32 | tf_op jit(solution)/shard_map/slice | solution.py:117
  40.5 0.6 slice.815
  44.1 1.0 multiply_reduce_fusion
  45.1 0.6 pad_maximum_fusion.4
  51.9 0.9 select_maximum_fusion
  52.8 1.0 slice.817
  53.8 1.2 %fusion.94 = (f32[12,6,18,128]{3,0,2,1:T(8,128)S(1)}, f32[12,6,18,128]{3,0,2,1:T(8,128)S(1)}, f32[12,6,18,128]{3,0,2,1:T(8,128)S(1)}, f32[12,6,18,128]{3,0,2,1:T(8,128)S(1)}, f32[12,6,18,128]{3,0,2,1:T(8,128)S(1)}) fusion(f32[18]{0:T(128)} %get-tuple-element.155, f32[12,6,128]{2,0,1:T(8,128)} %get-tuple-element.124, ...), kind=kLoop, calls=%fused_computation.195 | loop fusion | flops 995328 | bytes 4018320 | tf_op jit(solution)/shard_map/mul | solution.py:162
  55.4 0.8 slice_multiply_fusion.11
  56.8 0.8 slice_multiply_fusion.9
  58.3 0.8 slice_multiply_fusion.7
  62.5 0.6 fusion.106
  63.2 34.5 %all-gather.2.cloned.1.call-done = f32[4,56,36,128]{3,0,2,1:T(4,128)} async-done(((f32[4,7,36,128]{3,0,2,1:T(4,128)}), f32[4,56,36,128]{3,0,2,1:T(4,128)}) %all-gather.2.cloned.1.call-update) | async-done | bytes 4128784 | tf_op jit(solution)/shard_map/all_gather | solution.py:200
  97.6 2.2 %slice.954 = f32[4,8,6,36,128]{4,0,3,2,1:T(4,128)S(1)} slice(f32[4,8,7,36,128]{4,0,3,2,1:T(4,128)} %bitcast.61), slice={[0:4], [0:8], [0:6], [0:36], [0:128]} | slice | bytes 7077888 | tf_op jit(solution)/shard_map/slice | solution.py:203
  99.9 0.7 slice_bitcast_fusion
  101.6 3.8 %subtract_multiply_fusion = f32[4,14,36,128]{3,0,2,1:T(4,128)S(1)} fusion(s32[]{:T(128)S(6)} %select_n.216, s32[]{:T(128)S(6)} %select_n.215, f32[4,22,36,128]{3,0,2,1:T(4,128)S(1)} %pad_dynamic-slice_fusion.1, s32[]{:T(128)S(6)} %select_n.213, s32[]{:T(128)S(6)} %select_n.212, s32[]{:T(128)S(6)} %select_n.211, s32[]{:T(128)S(6)} %select_n.209, ...), kind=kLoop, calls=%fused_computation.28 | loop fusion | flops 5160960 | bytes 6193196 | tf_op jit(solution)/shard_map/mul | solution.py:130
  105.4 3.0 %fusion.93 = f32[4,6,36,128]{3,0,2,1:T(4,128)} fusion(f32[4,6,18,128]{3,0,2,1:T(4,128)S(1)} %get-tuple-element.129, f32[4,6,18,128]{3,0,2,1:T(4,128)S(1)} %get-tuple-element.128, f32[4,14,36,128]{3,0,2,1:T(4,128)S(1)} %subtract_multiply_fusion, s32[]{:T(128)S(6)} %select_n.224, s32[]{:T(128)S(6)} %select_n.223, s32[]{:T(128)S(6)} %select_n.221, ...), kind=kLoop, calls=%fused_computation.192 | loop fusion | flops 2322432 | bytes 2805800 | tf_op jit(solution)/shard_map/mul | solution.py:250
  (100 shorter events, 16.6 us)
Async XLA Ops:
  7.2 90.5 %all-gather.2.cloned.1.call-start = ((), (), s32[]{:S(2)}) async-start(), calls=%async_computation | async-start | bytes 4644864 | tf_op jit(solution)/shard_map/all_gather | solution.py:200
  11.1 29.2 %collective-permute-start.2 = (f32[4,7,18,128]{3,0,2,1:T(4,128)S(1)}, f32[4,7,18,128]{3,0,2,1:T(4,128)S(1)}, u32[]{:S(2)}, u32[]{:S(2)}) collective-permute-start(f32[4,7,18,128]{3,0,2,1:T(4,128)S(1)} %get-tuple-element.123), channel_id=1, source_target_pairs={{1,0},{2,1},{3,2},{4,3},{5,4},{6,5},{7,6},{8,7},{9,8},{10,9},{11,1... | collective-permute-start | bytes 774152 | tf_op jit(solution)/shard_map/ppermute | solution.py:26
  12.4 28.0 %collective-permute-start.3 = (f32[4,7,18,128]{3,0,2,1:T(4,128)S(1)}, f32[4,7,18,128]{3,0,2,1:T(4,128)S(1)}, u32[]{:S(2)}, u32[]{:S(2)}) collective-permute-start(f32[4,7,18,128]{3,0,2,1:T(4,128)S(1)} %get-tuple-element.123), channel_id=1, source_target_pairs={{2,0},{3,1},{4,2},{5,3},{6,4},{7,5},{8,6},{9,7},{10,8},{11,9},{12,... | collective-permute-start | bytes 774152 | tf_op jit(solution)/shard_map/ppermute | solution.py:26
  13.7 26.7 %collective-permute-start.1 = (f32[4,7,18,128]{3,0,2,1:T(4,128)S(1)}, f32[4,7,18,128]{3,0,2,1:T(4,128)S(1)}, u32[]{:S(2)}, u32[]{:S(2)}) collective-permute-start(f32[4,7,18,128]{3,0,2,1:T(4,128)S(1)} %get-tuple-element.122), channel_id=1, source_target_pairs={{0,2},{1,3},{2,4},{3,5},{4,6},{5,7},{6,8},{7,9},{8,10},{9,11},{10,... | collective-permute-start | bytes 774152 | tf_op jit(solution)/shard_map/ppermute | solution.py:26
  20.2 20.2 %collective-permute-start = (f32[4,7,18,128]{3,0,2,1:T(4,128)S(1)}, f32[4,7,18,128]{3,0,2,1:T(4,128)S(1)}, u32[]{:S(2)}, u32[]{:S(2)}) collective-permute-start(f32[4,7,18,128]{3,0,2,1:T(4,128)S(1)} %get-tuple-element.122), channel_id=1, source_target_pairs={{0,1},{1,2},{2,3},{3,4},{4,5},{5,6},{6,7},{7,8},{8,9},{9,10},{10,1... | collective-permute-start | bytes 774152 | tf_op jit(solution)/shard_map/ppermute | solution.py:26
  40.4 5.4 %copy-start.2 = (f32[4,7,18,128]{3,0,2,1:T(4,128)}, f32[4,7,18,128]{3,0,2,1:T(4,128)S(1)}, u32[]{:S(2)}) copy-start(f32[4,7,18,128]{3,0,2,1:T(4,128)S(1)} %collective-permute-done) | copy-start | bytes 774148
  40.4 6.1 %copy-start.1 = (f32[4,7,18,128]{3,0,2,1:T(4,128)}, f32[4,7,18,128]{3,0,2,1:T(4,128)S(1)}, u32[]{:S(2)}) copy-start(f32[4,7,18,128]{3,0,2,1:T(4,128)S(1)} %collective-permute-done.1) | copy-start | bytes 774148
  51.7 2.1 %slice-start = ((f32[4,7,18,128]{3,0,2,1:T(4,128)}), f32[4,6,18,128]{3,0,2,1:T(4,128)S(1)}, s32[]{:S(2)}) async-start(f32[4,7,18,128]{3,0,2,1:T(4,128)} %copy-done.1), calls=%async_computation.1 | async-start | bytes 442368 | tf_op jit(solution)/shard_map/slice | solution.py:224
  53.8 1.6 %copy-start.5 = (f32[11,128]{1,0:T(8,128)S(1)}, f32[11,128]{1,0:T(8,128)}, u32[]{:S(2)}) copy-start(f32[11,128]{1,0:T(8,128)} %slice.815) | copy-start | bytes 16900
  56.1 0.7 copy-start.4
  57.6 0.7 copy-start.3
  59.5 0.8 copy-start.8
  60.3 0.7 copy-start.7
  61.0 0.9 copy-start.6
  99.9 1.1 copy-start.9
  99.9 1.1 copy-start.10
  101.0 4.4 %copy-start = (f32[4,6,36,128]{3,0,2,1:T(4,128)S(1)}, f32[4,6,36,128]{3,0,2,1:T(4,128)}, u32[]{:S(2)}) copy-start(f32[4,6,36,128]{3,0,2,1:T(4,128)} %param.13) | copy-start | bytes 1327108
Sparse Core Ops, SparseCore 0:
  52.9 44.6 all-gather.1
where the time goes:
time: 116 us; the launch traced here: 115 us
  waiting for transfers between devices  34.5 us (30%)
  between operations  28 us (24%)
  other arithmetic  22.8 us (20%)
  local copies, waits for them, and re-layouts  17.7 us (15%)
  starting transfers between devices  12.3 us (11%)
    all_gather x1, waiting for transfers between devices, body(): lax.all_gather(jnp.concatenate([masked, slot], axis=1), 'freq', axis=1, t...  34.5 us
    ppermute x4, starting transfers between devices, from_neighbour(): return lax.ppermute(block, axis, pairs)  12.3 us
    mul x16, other arithmetic, propagate(): east_flux = east_speed[lo:hi] * spectrum  8.76 us
    slice x16, local copies, waits for them, and re-layouts, east_west(): behind = jnp.concatenate([zeros, east_flux[..., :-1]], axis=-1)  3.96 us
    mul x1, other arithmetic, source_change(): coupling * (centre * centre * (coef_plus * upper + coef_minus * lower) -...  3.76 us
    slice x6, local copies, waits for them, and re-layouts, propagate(): wet[lo + 1:hi, None, None, :]  3.61 us
    mul x1, other arithmetic, body(): return (wet_four * (moved + increment), orbital)  3.01 us
  transfers between devices with their start and end apart: 5, of which 1 were waited for; matrix products, arithmetic and copies ran while one was open for 11% of the time, Pallas kernels for 0%

commit v1 on v0

--- a/solution.py
+++ b/solution.py
@@ -3,6 +3,7 @@
 import jax.numpy as jnp
 from jax import lax
 from jax.sharding import PartitionSpec as P
+from jax.lax import axis_index, axis_size, ppermute
 
 FH = 4
 SUBSTEPS = 8
@@ -15,6 +16,22 @@
 coef_plus = 0.4096
 coef_minus = 3.1605
 coef_both = 2.589
+
+
+def convert_threads_in(block_in):
+    wide_n = axis_size("freq")
+    queue = tuple(((tick, (tick + 1) % wide_n) for tick in range(wide_n)))
+    t1, before = ([block_in], [block_in])
+    pages = tuple(((tick, (tick - 1) % wide_n) for tick in range(wide_n)))
+    for _ in range(wide_n // 2):
+        t1.append(ppermute(t1[-1], "freq", queue))
+    q = 0
+    while q < (wide_n - 1) // 2:
+        before.append(ppermute(before[-1], "freq", pages))
+        q += 1
+    clean = jnp.concatenate([*t1[::-1], *before[1:]], axis=1)
+    big = jnp.roll(clean, (axis_index("freq") - wide_n // 2) * block_in.shape[1], axis=1)
+    return big
 
 
 def from_neighbour(block, axis, distance, cyclic=False):
@@ -197,7 +214,7 @@
     freq_total = lax.axis_size("freq")
     slot = jnp.zeros((tile_rows, 1, dir_count, tile_cols), jnp.float32)
     slot = slot.at[:, 0, 0, :].set(partial_value)
-    gathered = lax.all_gather(jnp.concatenate([masked, slot], axis=1), "freq", axis=1, tiled=True)
+    gathered = convert_threads_in(jnp.concatenate([masked, slot], axis=1))
     gathered = gathered.reshape(tile_rows, freq_total, freq_count + 1, dir_count, tile_cols)
     partials = gathered[:, :, freq_count, 0, :]
     spectrum_all = gathered[:, :, :freq_count].reshape(

time: 116 us -> 96.5 us (0.83)
  the two profiles are of different devices: /device:TPU:1 before, /device:TPU:7 now
where the time goes in v1:
time: 96.5 us; the launch traced here: 95.9 us
  starting transfers between devices  29.1 us (30%)
  other arithmetic  20.5 us (21%)
  waiting for transfers between devices  20.4 us (21%)
  between operations  14.9 us (15%)
  local copies, waits for them, and re-layouts  10.9 us (11%)
    ppermute x4, starting transfers between devices, convert_threads_in(): t1.append(ppermute(t1[-1], 'freq', queue))  17.6 us
    ppermute x4, waiting for transfers between devices, convert_threads_in(): t1.append(ppermute(t1[-1], 'freq', queue))  16.4 us
    ppermute x4, starting transfers between devices, from_neighbour(): return lax.ppermute(block, axis, pairs)  11.5 us
    mul x16, other arithmetic, propagate(): east_flux = east_speed[lo:hi] * spectrum  7.69 us
    ppermute x3, waiting for transfers between devices, convert_threads_in(): before.append(ppermute(before[-1], 'freq', pages))  3.98 us
    slice x16, local copies, waits for them, and re-layouts, east_west(): behind = jnp.concatenate([zeros, east_flux[..., :-1]], axis=-1)  3.95 us
    mul x1, other arithmetic, source_change(): coupling * (centre * centre * (coef_plus * upper + coef_minus * lower) -...  3.94 us
    mul x1, other arithmetic, body(): return (wet_four * (moved + increment), orbital)  3.17 us
  transfers between devices with their start and end apart: 11, of which 4 were waited for; matrix products, arithmetic and copies ran while one was open for 18% of the time, Pallas kernels for 0%

profile of v1, /device:TPU:7, one launch (start us, length us, event | category | flops | bytes accessed | tf_op | source)
XLA Modules:
  0.0 95.9 jit_solution(4472078136862810695)
XLA Ops:
  0.6 0.7 convert_bitcast_fusion
  1.9 1.1 %fusion.159 = (f32[4,6,128]{2,0,1:T(4,128)S(1)}, f32[4,6,36,128]{3,0,2,1:T(4,128)S(1)}) fusion(f32[4,6,36,128]{3,0,2,1:T(4,128)} %param.13, f32[4,128]{1,0:T(4,128)S(1)} %get-tuple-element.135), kind=kLoop, calls=%fused_computation.314 | loop fusion | flops 218112 | bytes 899072 | tf_op jit(solution)/shard_map/reduce_sum | solution.py:212
  3.1 1.3 %constant_dynamic-update-slice_fusion.16 = f32[4,1,18,128]{3,0,2,1:T(4,128)S(1)} fusion(f32[4,1,18,128]{3,0,2,1:T(4,128)S(1)} %scatter.10, s32[]{:T(128)} %bitcast.2, f32[4,128]{1,0:T(4,128)} %param.14), kind=kLoop, calls=%fused_computation.276 | loop fusion | bytes 4100 | tf_op jit(solution)/shard_map/scatter | solution.py:206
  4.5 1.3 %collective-permute-start.2 = (f32[4,7,18,128]{3,0,2,1:T(4,128)S(1)}, f32[4,7,18,128]{3,0,2,1:T(4,128)S(1)}, u32[]{:S(2)}, u32[]{:S(2)}) collective-permute-start(f32[4,7,18,128]{3,0,2,1:T(4,128)S(1)} %get-tuple-element.123), channel_id=1, source_target_pairs={{1,0},{2,1},{3,2},{4,3},{5,4},{6,5},{7,6},{8,7},{9,8},{10,9},{11,1... | collective-permute-start | bytes 774152 | tf_op jit(solution)/shard_map/ppermute | solution.py:43
  5.8 1.3 %collective-permute-start.3 = (f32[4,7,18,128]{3,0,2,1:T(4,128)S(1)}, f32[4,7,18,128]{3,0,2,1:T(4,128)S(1)}, u32[]{:S(2)}, u32[]{:S(2)}) collective-permute-start(f32[4,7,18,128]{3,0,2,1:T(4,128)S(1)} %get-tuple-element.123), channel_id=1, source_target_pairs={{2,0},{3,1},{4,2},{5,3},{6,4},{7,5},{8,6},{9,7},{10,8},{11,9},{12,... | collective-permute-start | bytes 774152 | tf_op jit(solution)/shard_map/ppermute | solution.py:43
  7.1 4.0 %collective-permute-start = (f32[4,7,18,128]{3,0,2,1:T(4,128)S(1)}, f32[4,7,18,128]{3,0,2,1:T(4,128)S(1)}, u32[]{:S(2)}, u32[]{:S(2)}) collective-permute-start(f32[4,7,18,128]{3,0,2,1:T(4,128)S(1)} %get-tuple-element.122), channel_id=1, source_target_pairs={{0,1},{1,2},{2,3},{3,4},{4,5},{5,6},{6,7},{7,8},{8,9},{9,10},{10,1... | collective-permute-start | bytes 774152 | tf_op jit(solution)/shard_map/ppermute | solution.py:43
  11.1 4.9 %collective-permute-start.1 = (f32[4,7,18,128]{3,0,2,1:T(4,128)S(1)}, f32[4,7,18,128]{3,0,2,1:T(4,128)S(1)}, u32[]{:S(2)}, u32[]{:S(2)}) collective-permute-start(f32[4,7,18,128]{3,0,2,1:T(4,128)S(1)} %get-tuple-element.122), channel_id=1, source_target_pairs={{0,2},{1,3},{2,4},{3,5},{4,6},{5,7},{6,8},{7,9},{8,10},{9,11},{10,... | collective-permute-start | bytes 774152 | tf_op jit(solution)/shard_map/ppermute | solution.py:43
  16.3 1.4 %fusion.169 = (f32[1]{0:T(128)}, f32[1]{0:T(128)}) fusion(f32[2]{0:T(128)} %param.19), kind=kLoop, calls=%fused_computation.324 | loop fusion | bytes 16 | tf_op jit(solution)/shard_map/slice | solution.py:137
  17.7 1.5 %fusion.170 = (s32[1]{0:T(128)}, s32[1]{0:T(128)}, s32[1]{0:T(128)}, s32[1]{0:T(128)}) fusion(s32[4]{0:T(128)} %param.18), kind=kLoop, calls=%fused_computation.325 | loop fusion | bytes 32 | tf_op jit(solution)/shard_map/slice | solution.py:134
  33.0 1.0 %multiply_reduce_fusion = (f32[4,128]{1,0:T(4,128)S(1)}, f32[4,6,128]{2,0,1:T(4,128)S(1)}, f32[4,6,128]{2,0,1:T(4,128)S(1)}, f32[4,6,128]{2,0,1:T(4,128)S(1)}, f...) fusion(f32[4,6,128]{2,0,1:T(4,128)S(1)} %get-tuple-element.90, f32[6]{0:T(128)S(1)} %get-tuple-element.152, ...), kind=kLoop, calls=%fused_computation.254 | loop fusion | flops 340480 | bytes 86088 | tf_op jit(solution)/shard_map/reduce_sum | solution.py:212
  34.1 7.3 %collective-permute-start.4 = (f32[4,7,36,128]{3,0,2,1:T(4,128)S(1)}, f32[4,7,36,128]{3,0,2,1:T(4,128)S(1)}, u32[]{:S(2)}, u32[]{:S(2)}) collective-permute-start(f32[4,7,36,128]{3,0,2,1:T(4,128)S(1)} %pad_maximum_fusion.2), channel_id=1, source_target_pairs={{0,64},{64,128},{128,192},{192,256},{256,320},{320,384},{384,448},... | collective-permute-start | bytes 1548296 | tf_op jit(solution)/shard_map/ppermute | solution.py:27
  42.2 0.7 slice_multiply_fusion.11
  43.4 0.7 slice_multiply_fusion.9
  44.5 0.7 slice_multiply_fusion.7
  53.6 3.0 %collective-permute-start.5 = (f32[4,7,36,128]{3,0,2,1:T(4,128)S(1)}, f32[4,7,36,128]{3,0,2,1:T(4,128)S(1)}, u32[]{:S(2)}, u32[]{:S(2)}) collective-permute-start(f32[4,7,36,128]{3,0,2,1:T(4,128)S(1)} %collective-permute-done.4), channel_id=1, source_target_pairs={{0,64},{64,128},{128,192},{192,256},{256,320},{320,384},{384,448},... | collective-permute-start | bytes 1548296 | tf_op jit(solution)/shard_map/ppermute | solution.py:27
  57.0 5.5 %collective-permute-done.5 = f32[4,7,36,128]{3,0,2,1:T(4,128)S(1)} collective-permute-done((f32[4,7,36,128]{3,0,2,1:T(4,128)S(1)}, f32[4,7,36,128]{3,0,2,1:T(4,128)S(1)}, u32[]{:S(2)}, u32[]{:S(2)}) %collective-permute-start.5) | collective-permute-done | bytes 516128 | tf_op jit(solution)/shard_map/ppermute | solution.py:27
  62.6 3.7 %collective-permute-start.6 = (f32[4,7,36,128]{3,0,2,1:T(4,128)S(1)}, f32[4,7,36,128]{3,0,2,1:T(4,128)S(1)}, u32[]{:S(2)}, u32[]{:S(2)}) collective-permute-start(f32[4,7,36,128]{3,0,2,1:T(4,128)S(1)} %collective-permute-done.5), channel_id=1, source_target_pairs={{0,64},{64,128},{128,192},{192,256},{256,320},{320,384},{384,448},... | collective-permute-start | bytes 1548296 | tf_op jit(solution)/shard_map/ppermute | solution.py:27
  66.6 5.7 %collective-permute-done.6 = f32[4,7,36,128]{3,0,2,1:T(4,128)S(1)} collective-permute-done((f32[4,7,36,128]{3,0,2,1:T(4,128)S(1)}, f32[4,7,36,128]{3,0,2,1:T(4,128)S(1)}, u32[]{:S(2)}, u32[]{:S(2)}) %collective-permute-start.6) | collective-permute-done | bytes 516128 | tf_op jit(solution)/shard_map/ppermute | solution.py:27
  72.3 3.7 %collective-permute-start.7 = (f32[4,7,36,128]{3,0,2,1:T(4,128)S(1)}, f32[4,7,36,128]{3,0,2,1:T(4,128)S(1)}, u32[]{:S(2)}, u32[]{:S(2)}) collective-permute-start(f32[4,7,36,128]{3,0,2,1:T(4,128)S(1)} %collective-permute-done.6), channel_id=1, source_target_pairs={{0,64},{64,128},{128,192},{192,256},{256,320},{320,384},{384,448},... | collective-permute-start | bytes 1548296 | tf_op jit(solution)/shard_map/ppermute | solution.py:27
  76.8 5.2 %collective-permute-done.7 = f32[4,7,36,128]{3,0,2,1:T(4,128)S(1)} collective-permute-done((f32[4,7,36,128]{3,0,2,1:T(4,128)S(1)}, f32[4,7,36,128]{3,0,2,1:T(4,128)S(1)}, u32[]{:S(2)}, u32[]{:S(2)}) %collective-permute-start.7) | collective-permute-done | bytes 516128 | tf_op jit(solution)/shard_map/ppermute | solution.py:27
  82.5 4.0 %collective-permute-done.10 = f32[4,7,36,128]{3,0,2,1:T(4,128)S(1)} collective-permute-done((f32[4,7,36,128]{3,0,2,1:T(4,128)S(1)}, f32[4,7,36,128]{3,0,2,1:T(4,128)S(1)}, u32[]{:S(2)}, u32[]{:S(2)}) %collective-permute-start.10) | collective-permute-done | bytes 516128 | tf_op jit(solution)/shard_map/ppermute | solution.py:30
  88.2 0.6 multiply_add_fusion
  88.8 3.9 %subtract_multiply_fusion = f32[4,14,36,128]{3,0,2,1:T(4,128)S(1)} fusion(s32[]{:T(128)S(6)} %select_n.230, s32[]{:T(128)S(6)} %select_n.229, f32[4,22,36,128]{3,0,2,1:T(4,128)S(1)} %pad_dynamic-slice_fusion.1, s32[]{:T(128)S(6)} %select_n.227, s32[]{:T(128)S(6)} %select_n.226, s32[]{:T(128)S(6)} %select_n.225, s32[]{:T(128)S(6)} %select_n.223, ...), kind=kLoop, calls=%fused_computation.28 | loop fusion | flops 5160960 | bytes 6193196 | tf_op jit(solution)/shard_map/mul | solution.py:147
  92.8 3.2 %fusion.93 = f32[4,6,36,128]{3,0,2,1:T(4,128)} fusion(f32[4,6,36,128]{3,0,2,1:T(4,128)S(1)} %get-tuple-element.91, f32[4,6,18,128]{3,0,2,1:T(4,128)S(1)} %get-tuple-element.129, f32[4,6,18,128]{3,0,2,1:T(4,128)S(1)} %get-tuple-element.128, f32[4,14,36,128]{3,0,2,1:T(4,128)S(1)} %subtract_multiply_fusion, s32[]{:T(128)S(6)} %select_n.238, s32[]{:T(128)S(6)} %select_n.237, ...), kind=kLoop, calls=%fused_computation.191 | loop fusion | flops 2211840 | bytes 2805800 | tf_op jit(solution)/shard_map/mul | solution.py:267
  (112 shorter events, 14.6 us)
Async XLA Ops:
  4.5 28.2 %collective-permute-start.2 = (f32[4,7,18,128]{3,0,2,1:T(4,128)S(1)}, f32[4,7,18,128]{3,0,2,1:T(4,128)S(1)}, u32[]{:S(2)}, u32[]{:S(2)}) collective-permute-start(f32[4,7,18,128]{3,0,2,1:T(4,128)S(1)} %get-tuple-element.123), channel_id=1, source_target_pairs={{1,0},{2,1},{3,2},{4,3},{5,4},{6,5},{7,6},{8,7},{9,8},{10,9},{11,1... | collective-permute-start | bytes 774152 | tf_op jit(solution)/shard_map/ppermute | solution.py:43
  5.8 27.0 %collective-permute-start.3 = (f32[4,7,18,128]{3,0,2,1:T(4,128)S(1)}, f32[4,7,18,128]{3,0,2,1:T(4,128)S(1)}, u32[]{:S(2)}, u32[]{:S(2)}) collective-permute-start(f32[4,7,18,128]{3,0,2,1:T(4,128)S(1)} %get-tuple-element.123), channel_id=1, source_target_pairs={{2,0},{3,1},{4,2},{5,3},{6,4},{7,5},{8,6},{9,7},{10,8},{11,9},{12,... | collective-permute-start | bytes 774152 | tf_op jit(solution)/shard_map/ppermute | solution.py:43
  7.1 25.6 %collective-permute-start = (f32[4,7,18,128]{3,0,2,1:T(4,128)S(1)}, f32[4,7,18,128]{3,0,2,1:T(4,128)S(1)}, u32[]{:S(2)}, u32[]{:S(2)}) collective-permute-start(f32[4,7,18,128]{3,0,2,1:T(4,128)S(1)} %get-tuple-element.122), channel_id=1, source_target_pairs={{0,1},{1,2},{2,3},{3,4},{4,5},{5,6},{6,7},{7,8},{8,9},{9,10},{10,1... | collective-permute-start | bytes 774152 | tf_op jit(solution)/shard_map/ppermute | solution.py:43
  11.1 21.7 %collective-permute-start.1 = (f32[4,7,18,128]{3,0,2,1:T(4,128)S(1)}, f32[4,7,18,128]{3,0,2,1:T(4,128)S(1)}, u32[]{:S(2)}, u32[]{:S(2)}) collective-permute-start(f32[4,7,18,128]{3,0,2,1:T(4,128)S(1)} %get-tuple-element.122), channel_id=1, source_target_pairs={{0,2},{1,3},{2,4},{3,5},{4,6},{5,7},{6,8},{7,9},{8,10},{9,11},{10,... | collective-permute-start | bytes 774152 | tf_op jit(solution)/shard_map/ppermute | solution.py:43
  34.1 19.4 %collective-permute-start.4 = (f32[4,7,36,128]{3,0,2,1:T(4,128)S(1)}, f32[4,7,36,128]{3,0,2,1:T(4,128)S(1)}, u32[]{:S(2)}, u32[]{:S(2)}) collective-permute-start(f32[4,7,36,128]{3,0,2,1:T(4,128)S(1)} %pad_maximum_fusion.2), channel_id=1, source_target_pairs={{0,64},{64,128},{128,192},{192,256},{256,320},{320,384},{384,448},... | collective-permute-start | bytes 1548296 | tf_op jit(solution)/shard_map/ppermute | solution.py:27
  41.4 25.2 %collective-permute-start.8 = (f32[4,7,36,128]{3,0,2,1:T(4,128)S(1)}, f32[4,7,36,128]{3,0,2,1:T(4,128)S(1)}, u32[]{:S(2)}, u32[]{:S(2)}) collective-permute-start(f32[4,7,36,128]{3,0,2,1:T(4,128)S(1)} %pad_maximum_fusion.2), channel_id=1, source_target_pairs={{0,448},{64,0},{128,64},{192,128},{256,192},{320,256},{384,320},{4... | collective-permute-start | bytes 1548296 | tf_op jit(solution)/shard_map/ppermute | solution.py:30
  53.6 9.0 %collective-permute-start.5 = (f32[4,7,36,128]{3,0,2,1:T(4,128)S(1)}, f32[4,7,36,128]{3,0,2,1:T(4,128)S(1)}, u32[]{:S(2)}, u32[]{:S(2)}) collective-permute-start(f32[4,7,36,128]{3,0,2,1:T(4,128)S(1)} %collective-permute-done.4), channel_id=1, source_target_pairs={{0,64},{64,128},{128,192},{192,256},{256,320},{320,384},{384,448},... | collective-permute-start | bytes 1548296 | tf_op jit(solution)/shard_map/ppermute | solution.py:27
  62.6 9.7 %collective-permute-start.6 = (f32[4,7,36,128]{3,0,2,1:T(4,128)S(1)}, f32[4,7,36,128]{3,0,2,1:T(4,128)S(1)}, u32[]{:S(2)}, u32[]{:S(2)}) collective-permute-start(f32[4,7,36,128]{3,0,2,1:T(4,128)S(1)} %collective-permute-done.5), channel_id=1, source_target_pairs={{0,64},{64,128},{128,192},{192,256},{256,320},{320,384},{384,448},... | collective-permute-start | bytes 1548296 | tf_op jit(solution)/shard_map/ppermute | solution.py:27
  66.6 10.2 %collective-permute-start.9 = (f32[4,7,36,128]{3,0,2,1:T(4,128)S(1)}, f32[4,7,36,128]{3,0,2,1:T(4,128)S(1)}, u32[]{:S(2)}, u32[]{:S(2)}) collective-permute-start(f32[4,7,36,128]{3,0,2,1:T(4,128)S(1)} %collective-permute-done.8), channel_id=1, source_target_pairs={{0,448},{64,0},{128,64},{192,128},{256,192},{320,256},{384,320},{4... | collective-permute-start | bytes 1548296 | tf_op jit(solution)/shard_map/ppermute | solution.py:30
  72.3 9.7 %collective-permute-start.7 = (f32[4,7,36,128]{3,0,2,1:T(4,128)S(1)}, f32[4,7,36,128]{3,0,2,1:T(4,128)S(1)}, u32[]{:S(2)}, u32[]{:S(2)}) collective-permute-start(f32[4,7,36,128]{3,0,2,1:T(4,128)S(1)} %collective-permute-done.6), channel_id=1, source_target_pairs={{0,64},{64,128},{128,192},{192,256},{256,320},{320,384},{384,448},... | collective-permute-start | bytes 1548296 | tf_op jit(solution)/shard_map/ppermute | solution.py:27
  76.8 9.7 %collective-permute-start.10 = (f32[4,7,36,128]{3,0,2,1:T(4,128)S(1)}, f32[4,7,36,128]{3,0,2,1:T(4,128)S(1)}, u32[]{:S(2)}, u32[]{:S(2)}) collective-permute-start(f32[4,7,36,128]{3,0,2,1:T(4,128)S(1)} %collective-permute-done.9), channel_id=1, source_target_pairs={{0,448},{64,0},{128,64},{192,128},{256,192},{320,256},{384,320},{4... | collective-permute-start | bytes 1548296 | tf_op jit(solution)/shard_map/ppermute | solution.py:30
  87.2 1.0 %copy-start = (s32[4,128]{1,0:T(4,128)S(1)}, s32[4,128]{1,0:T(4,128)}, u32[]{:S(2)}) copy-start(s32[4,128]{1,0:T(4,128)} %param.16) | copy-start | bytes 6148
  87.2 1.0 %copy-start.1 = (f32[4,128]{1,0:T(4,128)S(1)}, f32[4,128]{1,0:T(4,128)}, u32[]{:S(2)}) copy-start(f32[4,128]{1,0:T(4,128)} %param.17) | copy-start | bytes 6148
